TPU v7x, 32 devices: a whole 2x2x4 slice. The times are simulated.
32 devices in a mesh: tm: 8 (over z, y), cal: 4 (over x, core).
Axes of the slice: x: 2, y: 2, z: 4, core: 2. Of those that a mesh axis runs over, the one named last changes fastest.
Arguments:
- src_design: float32 [5, 4096, 128], P(None, ('tm', 'cal')), may hold values from -6 to 6
- att_design: float32 [3, 4096, 128], P(None, ('tm', 'cal')), may hold values from -6 to 6
- obs_phase: float32 [4096, 128], P(('tm', 'cal')), may hold values from 0 to 1
- cal_design: float32 [4096, 128], P(('tm', 'cal')), may hold values from -6 to 6
- obs_weight: float32 [4096, 128], P(('tm', 'cal')), may hold values from 0.1 to 12
- knot_index: int32 [4096, 128], P(('tm', 'cal')), may hold values from 0 to 4092, as said below
- cal_block: int32 [4096, 128], P(('tm', 'cal')), may hold values from 0 to 7
- cal_column: int32 [4096, 128], P(('tm', 'cal')), may hold values from 0 to 4095
- obs_count: int32 [4096], P(('tm', 'cal')), may hold values from 32 to 128
- src_res: float32 [5, 4096], P(None, ('tm', 'cal')), may hold values from -6 to 6
- att_res: float32 [3, 4096], P(None, ('tm', 'cal')), may hold values from -6 to 6
- cal_res: float32 [8, 4096], P('cal'), may hold values from -6 to 6
- src_dir: float32 [5, 4096], P(None, ('tm', 'cal')), may hold values from -6 to 6
- att_dir: float32 [3, 4096], P(None, ('tm', 'cal')), may hold values from -6 to 6
- cal_dir: float32 [8, 4096], P('cal'), may hold values from -6 to 6
Outputs:
- new_src_res: float32 [5, 4096], P(None, ('tm', 'cal'))
- new_att_res: float32 [3, 4096], P(None, ('tm', 'cal'))
- new_cal_res: float32 [8, 4096], P('cal')
- new_src_dir: float32 [5, 4096], P(None, ('tm', 'cal'))
- new_att_dir: float32 [3, 4096], P(None, ('tm', 'cal'))
- new_cal_dir: float32 [8, 4096], P('cal')
Inputs may be any that keep to these rules, and one draw needn't show every extreme that they name: The observations of source row s have knot intervals from (s // 128) * 128 to (s // 128) * 128 + 127, and knot_index + 3 < 4096.
All inputs are finite; a program needn't handle non-finite values.
Results may differ from a plain program's by a relative error of at most 0.00015.
Values sent between devices are 32-bit elements; how exact they have to be, the bound alone decides.
No kernel may reach another device: no remote copies, remote signals or barrier semaphores. Data moves between devices by JAX's collectives and lax.ppermute only.
A program may use at most 64 MiB of HBM per device.

v0:
```python
import jax
import jax.numpy as jnp
from jax import lax
from jax.sharding import PartitionSpec as P

EXACT = lax.Precision.HIGHEST


def passed_along(block, axis, distance):
    devices = range(lax.axis_size(axis))
    route = [(i - distance, i) for i in devices if i - distance in devices]
    return lax.ppermute(block, axis, route)


def spline(phase):
    rest = 1.0 - phase
    cube = phase * phase * phase
    square = phase * phase
    first = rest * rest * rest / 6.0
    second = (3.0 * cube - 6.0 * square + 4.0) / 6.0
    third = (-3.0 * cube + 3.0 * square + 3.0 * phase + 1.0) / 6.0
    fourth = cube / 6.0
    return (first, second, third, fourth)


def local(
    src_design,
    att_design,
    obs_phase,
    cal_design,
    obs_weight,
    knot_index,
    cal_block,
    cal_column,
    obs_count,
    src_res,
    att_res,
    cal_res,
    src_dir,
    att_dir,
    cal_dir,
):
    knot_count = att_dir.shape[1]
    blocks, col_width = cal_dir.shape
    all_blocks = blocks * lax.axis_size("cal")
    cal_size = all_blocks * col_width
    lane = 128
    rows = cal_size // lane
    src_rows, slots = obs_phase.shape
    first_row = (lax.axis_index("tm") == 0).astype(jnp.float32)
    cal_values = lax.all_gather(cal_dir, "cal", axis=0, tiled=True)
    edge_knots = passed_along(att_dir[:, :3], ("tm", "cal"), -1)
    att_ext = jnp.concatenate([att_dir, edge_knots], axis=1)
    live_mask = (lax.broadcasted_iota(jnp.int32, obs_phase.shape, 1) < obs_count[:, None]).astype(
        jnp.float32
    )
    basis = spline(obs_phase)
    local_knot = knot_index - lax.axis_index(("tm", "cal")) * knot_count
    knot_iota = lax.broadcasted_iota(jnp.int32, (knot_count, 1, 1), 0)
    knot_hot = (local_knot[None] == knot_iota).astype(jnp.float32)
    table = jnp.stack([att_ext[:, m : m + knot_count].T for m in range(4)], axis=1)
    table = table.reshape(knot_count, 12)
    picked = jnp.einsum("jq,jso->qso", table, knot_hot, precision=EXACT).reshape(
        4, 3, src_rows, slots
    )
    y_att = jnp.zeros_like(obs_phase)
    for m in range(4):
        y_att = y_att + basis[m] * jnp.sum(att_design * picked[m], axis=0)
    flat_index = cal_block * col_width + cal_column
    high = flat_index // lane
    low = flat_index % lane
    high_hot = (high[None] == lax.broadcasted_iota(jnp.int32, (rows, 1, 1), 0)).astype(jnp.float32)
    low_hot = (low[None] == lax.broadcasted_iota(jnp.int32, (lane, 1, 1), 0)).astype(jnp.float32)
    cal_table = cal_values.reshape(rows, lane)
    row_vals = jnp.einsum("hl,hso->lso", cal_table, high_hot, precision=EXACT)
    y_cal = cal_design * jnp.sum(row_vals * low_hot, axis=0)
    y_src = jnp.sum(src_design * src_dir[:, :, None], axis=0)
    response = live_mask * (y_src + y_att + y_cal)
    weighted = obs_weight * response
    curv_local = jnp.sum(weighted * response)
    norm_local = (
        jnp.sum(src_res * src_res)
        + jnp.sum(att_res * att_res)
        + first_row * jnp.sum(cal_res * cal_res)
    )
    q_src = jnp.sum(src_design * weighted[None], axis=2)
    scaled = att_design * weighted[None]
    spread = jnp.stack([basis[m][None] * scaled for m in range(4)], axis=0).reshape(
        12, src_rows, slots
    )
    gathered = jnp.einsum("qso,jso->jq", spread, knot_hot, precision=EXACT).reshape(
        knot_count, 4, 3
    )
    grad_ext = jnp.zeros((3, knot_count + 3), jnp.float32)
    for m in range(4):
        grad_ext = grad_ext + jnp.pad(gathered[:, m, :].T, ((0, 0), (m, 3 - m)))
    incoming = passed_along(grad_ext[:, knot_count:], ("tm", "cal"), 1)
    q_att = jnp.concatenate([grad_ext[:, :3] + incoming, grad_ext[:, 3:knot_count]], axis=1)
    cal_weighted = (cal_design * weighted)[None] * low_hot
    cal_term = jnp.einsum("hso,lso->hl", high_hot, cal_weighted, precision=EXACT)
    scalars = jnp.zeros((1, lane), jnp.float32).at[0, 0].set(norm_local).at[0, 1].set(curv_local)
    packed = jnp.concatenate([cal_term, scalars], axis=0)
    summed = lax.psum(packed, ("tm", "cal"))
    norm_now = summed[rows, 0]
    curvature = summed[rows, 1]
    own = lax.axis_index("cal") * (blocks * col_width // lane)
    q_cal = lax.dynamic_slice_in_dim(summed, own, blocks * col_width // lane, 0).reshape(
        blocks, col_width
    )
    step_len = norm_now / curvature
    new_src_res = src_res - step_len * q_src
    new_att_res = att_res - step_len * q_att
    new_cal_res = cal_res - step_len * q_cal
    next_local = (
        jnp.sum(new_src_res * new_src_res)
        + jnp.sum(new_att_res * new_att_res)
        + first_row * jnp.sum(new_cal_res * new_cal_res)
    )
    norm_next = lax.psum(jnp.zeros((1, lane), jnp.float32).at[0, 0].set(next_local), ("tm", "cal"))[
        0, 0
    ]
    ratio = norm_next / norm_now
    return (
        new_src_res,
        new_att_res,
        new_cal_res,
        new_src_res + ratio * src_dir,
        new_att_res + ratio * att_dir,
        new_cal_res + ratio * cal_dir,
    )


def solution(mesh):
    return jax.shard_map(
        local,
        mesh=mesh,
        in_specs=(
            P(None, ("tm", "cal"), None),
            P(None, ("tm", "cal"), None),
            P(("tm", "cal"), None),
            P(("tm", "cal"), None),
            P(("tm", "cal"), None),
            P(("tm", "cal"), None),
            P(("tm", "cal"), None),
            P(("tm", "cal"), None),
            P(("tm", "cal")),
            P(None, ("tm", "cal")),
            P(None, ("tm", "cal")),
            P("cal", None),
            P(None, ("tm", "cal")),
            P(None, ("tm", "cal")),
            P("cal", None),
        ),
        out_specs=(
            P(None, ("tm", "cal")),
            P(None, ("tm", "cal")),
            P("cal", None),
            P(None, ("tm", "cal")),
            P(None, ("tm", "cal")),
            P("cal", None),
        ),
        check_vma=False,
    )
```

profile of v0, /device:TPU:0, one launch (start us, length us, event | category | flops | bytes accessed | tf_op | source)
XLA Modules:
  0.0 323.5 jit_solution(16515309153429786869)
XLA Ops:
  7.2 1.3 collective-permute-start
  8.5 0.6 compare_reduce_fusion.1
  9.2 0.6 compare_reduce_fusion
  9.8 0.7 constant_dynamic-update-slice_fusion.1
  10.5 1.4 multiply_reduce_fusion.4
  11.9 1.3 multiply_reduce_fusion.8
  13.2 1.3 multiply_reduce_fusion.6
  17.7 0.8 broadcast_subtract_fusion
  18.6 7.7 %all-gather = f32[4,2,4096]{2,1,0:T(2,128)S(1)} all-gather(f32[1,2,4096]{2,1,0:T(2,128)} %bitcast.78), channel_id=1, replica_groups=mesh['tm'=8,'cal'=4] {'cal'}, dimensions={0}, use_global_device_ids=true | all-gather | bytes 163840 | tf_op jit(solution)/shard_map/all_gather | solution.py:51
  26.4 0.9 add_select_fusion.1
  27.4 1.3 iota_compare_fusion.1
  28.7 38.5 %copy.50 = pred[128,128,128]{2,0,1:T(32,128)(4,1)S(1)} copy(pred[128,128,128]{1,0,2:T(32,128)(4,1)S(1)} %iota_compare_fusion.1) | data formatting | bytes 4194304 | tf_op jit(solution)/shard_map/eq | solution.py:60
  67.2 2.7 iota_compare_fusion
  70.0 20.5 %copy.55 = pred[256,128,128]{2,0,1:T(32,128)(4,1)} copy(pred[256,128,128]{1,0,2:T(32,128)(4,1)S(1)} %iota_compare_fusion) | data formatting | bytes 8388608 | tf_op jit(solution)/shard_map/eq | solution.py:72
  90.7 8.2 %fusion = f32[128,128]{1,0:T(8,128)S(1)} fusion(s32[128,128]{1,0:T(8,128)S(1)} %get-tuple-element.62, pred[256,128,128]{2,0,1:T(32,128)(4,1)} %copy.55, f32[256,128]{1,0:T(8,128)S(1)} %reshape.140), kind=kOutput, calls=%fused_computation.2 | convolution fusion | flops 6448726016 | bytes 4456448 | tf_op jit(solution)/shard_map/hl,hso->lso/dot_general | solution.py:75
  99.1 2.2 fusion.29
  101.3 0.8 fusion.7
  102.9 4.2 %fusion.4 = f32[128,4,3]{0,1,2:T(4,128)S(1)} fusion(f32[4,3,128,128]{3,0,2,1:T(4,128)S(1)} %copy.59, s32[128,128]{0,1:T(8,128)S(1)} %copy.49), kind=kOutput, calls=%fused_computation.9 | convolution fusion | flops 304087040 | bytes 858112 | tf_op jit(solution)/shard_map/qso,jso->jq/dot_general | solution.py:91
  107.9 2.2 collective-permute-start.1
  110.1 4.7 %fusion.1 = f32[128,128,128]{2,0,1:T(8,128)} fusion(f32[128,128]{1,0:T(8,128)S(1)} %get-tuple-element.52, s32[128,128]{1,0:T(8,128)S(1)} %get-tuple-element.62), kind=kLoop, calls=%fused_computation.5 | loop fusion | flops 4194304 | bytes 8519680 | tf_op jit(solution)/shard_map/mul | solution.py:99
  114.8 9.3 %copy.57 = f32[128,128,128]{1,0,2:T(8,128)} copy(f32[128,128,128]{2,0,1:T(8,128)} %fusion.1) | data formatting | bytes 16777216 | tf_op jit(solution)/shard_map/mul | solution.py:99
  124.2 11.2 %convolution_bitcast_fusion = f32[256,128]{1,0:T(8,128)S(1)} fusion(f32[128,128,128]{1,0,2:T(8,128)} %copy.57, s32[128,128]{0,1:T(8,128)S(1)} %copy.48), kind=kOutput, calls=%fused_computation.8 | convolution fusion | flops 6446645248 | bytes 8585216 | tf_op jit(solution)/shard_map/hso,lso->hl/dot_general | solution.py:100
  135.3 2.5 fusion.28
  137.9 1.4 scatter.11
  139.3 0.7 pad_maximum_fusion
  140.0 123.3 %all-reduce.8.cloned.1.call-done = f32[257,128]{1,0:T(8,128)} async-done(((f32[257,128]{1,0:T(8,128)}), f32[257,128]{1,0:T(8,128)}) %all-reduce.8.cloned.1.call-update) | async-done | bytes 131600 | tf_op jit(solution)/shard_map/psum | solution.py:103
  263.3 1.3 fusion.26
  266.0 0.8 dynamic-slice_multiply_fusion
  267.4 0.7 multiply_reduce_fusion.3
  268.8 0.8 multiply_reduce_fusion.7
  271.6 42.5 %psum.15 = f32[1,128]{1,0:T(1,128)S(1)} all-reduce(f32[1,128]{1,0:T(1,128)S(1)} %scatter.14), channel_id=1, replica_groups=mesh['tm'=8,'cal'=4] {'tm','cal'}, use_global_device_ids=true, to_apply=%region_17.18 | all-reduce | flops 128 | bytes 1024 | tf_op jit(solution)/shard_map/psum | solution.py:119
  316.0 0.6 multiply_add_fusion.1
  (63 shorter events, 4.6 us)
Async XLA Ops:
  7.2 256.2 %all-reduce.8.cloned.1.call-start = ((), (), s32[]{:S(2)}) async-start(), calls=%async_computation | async-start | bytes 270336 | tf_op jit(solution)/shard_map/psum | solution.py:103
  7.2 91.8 %collective-permute-start = (f32[3,3]{1,0:T(4,128)}, f32[3,3]{1,0:T(4,128)S(1)}, u32[]{:S(2)}, u32[]{:S(2)}) collective-permute-start(f32[3,3]{1,0:T(4,128)} %bitcast.79), channel_id=1, source_target_pairs={{1,0},{2,1},{3,2},{4,3},{5,4},{6,5},{7,6},{8,7},{9,8},{10,9},{11,1... | collective-permute-start | bytes 116 | tf_op jit(solution)/shard_map/ppermute | solution.py:12
  69.9 20.6 %copy-start = (f32[5,128,128]{2,1,0:T(8,128)S(1)}, f32[5,128,128]{2,1,0:T(8,128)}, u32[]{:S(2)}) copy-start(f32[5,128,128]{2,1,0:T(8,128)} %param.21) | copy-start | bytes 983044
  69.9 20.6 %copy-start.9 = (f32[5,128]{1,0:T(8,128)S(1)}, f32[5,128]{1,0:T(8,128)}, u32[]{:S(2)}) copy-start(f32[5,128]{1,0:T(8,128)} %param.33) | copy-start | bytes 7684
  90.7 8.4 %copy-start.8 = (f32[3,128]{1,0:T(4,128)S(1)}, f32[3,128]{1,0:T(4,128)}, u32[]{:S(2)}) copy-start(f32[3,128]{1,0:T(4,128)} %param.34) | copy-start | bytes 4612
  90.7 10.6 %copy-start.1 = (f32[3,128,128]{2,1,0:T(8,128)S(1)}, f32[3,128,128]{2,1,0:T(8,128)}, u32[]{:S(2)}) copy-start(f32[3,128,128]{2,1,0:T(8,128)} %param.22) | copy-start | bytes 589828
  98.9 3.2 copy-start.5
  98.9 3.2 copy-start.6
  98.9 3.2 copy-start.7
  99.0 3.2 copy-start.14
  107.9 32.1 %collective-permute-start.1 = (f32[3,3]{1,0:T(4,128)S(1)}, f32[3,3]{1,0:T(4,128)S(1)}, u32[]{:S(2)}, u32[]{:S(2)}) collective-permute-start(f32[3,3]{1,0:T(4,128)S(1)} %slice.142), channel_id=1, source_target_pairs={{0,1},{1,2},{2,3},{3,4},{4,5},{5,6},{6,7},{7,8},{8,9},{9,10},{10,1... | collective-permute-start | bytes 116 | tf_op jit(solution)/shard_map/ppermute | solution.py:12
  124.2 142.6 %copy-start.11 = (f32[5,128]{1,0:T(8,128)S(1)}, f32[5,128]{1,0:T(8,128)}, u32[]{:S(2)}) copy-start(f32[5,128]{1,0:T(8,128)} %param.30) | copy-start | bytes 7684
  124.2 143.3 %copy-start.4 = (f32[2,4096]{1,0:T(2,128)S(1)}, f32[2,4096]{1,0:T(2,128)}, u32[]{:S(2)}) copy-start(f32[2,4096]{1,0:T(2,128)} %param.32) | copy-start | bytes 98308
  124.2 144.7 %copy-start.12 = (f32[3,128]{1,0:T(4,128)S(1)}, f32[3,128]{1,0:T(4,128)}, u32[]{:S(2)}) copy-start(f32[3,128]{1,0:T(4,128)} %param.31) | copy-start | bytes 4612
  124.2 191.8 %copy-start.2 = (f32[2,4096]{1,0:T(2,128)S(1)}, f32[2,4096]{1,0:T(2,128)}, u32[]{:S(2)}) copy-start(f32[2,4096]{1,0:T(2,128)} %param.35) | copy-start | bytes 98308
  267.4 49.2 %copy-start.10 = (f32[5,128]{1,0:T(8,128)}, f32[5,128]{1,0:T(8,128)S(1)}, u32[]{:S(2)}) copy-start(f32[5,128]{1,0:T(8,128)S(1)} %get-tuple-element.51) | copy-start | bytes 7684
  268.1 48.5 %copy-start.3 = (f32[2,4096]{1,0:T(2,128)}, f32[2,4096]{1,0:T(2,128)S(1)}, u32[]{:S(2)}) copy-start(f32[2,4096]{1,0:T(2,128)S(1)} %get-tuple-element.47) | copy-start | bytes 98308
  269.6 47.1 %copy-start.13 = (f32[3,128]{1,0:T(4,128)}, f32[3,128]{1,0:T(4,128)S(1)}, u32[]{:S(2)}) copy-start(f32[3,128]{1,0:T(4,128)S(1)} %get-tuple-element.49) | copy-start | bytes 4612
Sparse Core Ops, SparseCore 0:
  140.1 123.1 all-reduce.7
where the time goes:
time: 324 us
  waiting for transfers between devices  123 us (38%)
  local copies, waits for them, and re-layouts  73.3 us (23%)
  blocking collectives  50.1 us (15%)
  matrix products  25.8 us (8%)
  other arithmetic  25.7 us (8%)
  between operations  21.7 us (7%)
  starting transfers between devices  3.56 us (1%)
    psum x1, waiting for transfers between devices, local(): summed = lax.psum(packed, ('tm', 'cal'))  123 us
    psum x1, blocking collectives, local(): lax.psum(jnp.zeros((1, lane), jnp.float32).at[0, 0].set(next_local), ('tm...  42.5 us
    eq x1, local copies, waits for them, and re-layouts, local(): knot_hot = (local_knot[None] == knot_iota).astype(jnp.float32)  38.5 us
    eq x1, local copies, waits for them, and re-layouts, local(): high[None] == lax.broadcasted_iota(jnp.int32, (rows, 1, 1), 0)  20.5 us
    dot_general x1, matrix products, local(): jnp.einsum('hso,lso->hl', high_hot, cal_weighted, precision=EXACT)  11.2 us
    mul x1, local copies, waits for them, and re-layouts, local(): cal_weighted = (cal_design * weighted)[None] * low_hot  9.32 us
    dot_general x1, matrix products, local(): row_vals = jnp.einsum('hl,hso->lso', cal_table, high_hot, precision=EXACT)  8.23 us
    all_gather x1, blocking collectives, local(): cal_values = lax.all_gather(cal_dir, 'cal', axis=0, tiled=True)  7.65 us
  transfers between devices with their start and end apart: 3, of which 1 were waited for; matrix products, arithmetic and copies ran while one was open for 34% of the time, Pallas kernels for 0%

commit v1 on v0

--- a/solution.py
+++ b/solution.py
@@ -4,6 +4,7 @@
 from jax.sharding import PartitionSpec as P
 
 EXACT = lax.Precision.HIGHEST
+_render_zones = lambda vals: jax.lax.all_gather(vals, axis_name=("tm", "cal")).sum(axis=0)
 
 
 def passed_along(block, axis, distance):
@@ -116,9 +117,7 @@
         + jnp.sum(new_att_res * new_att_res)
         + first_row * jnp.sum(new_cal_res * new_cal_res)
     )
-    norm_next = lax.psum(jnp.zeros((1, lane), jnp.float32).at[0, 0].set(next_local), ("tm", "cal"))[
-        0, 0
-    ]
+    norm_next = _render_zones(jnp.zeros((1, lane), jnp.float32).at[0, 0].set(next_local))[0, 0]
     ratio = norm_next / norm_now
     return (
         new_src_res,

time: 324 us -> 324 us (level)
    all_gather x0 -> x1, blocking collectives: none -> 42.5 us  [jax.lax.all_gather(vals, axis_name=('tm', 'cal')).sum(axis=0)]
    psum x1 -> x0, blocking collectives: 42.5 us -> none  [local(): lax.psum(jnp.zeros((1, lane), jnp.float32).at[0, 0].set(next_local), ('tm...]
where the time goes in v1:
time: 324 us
  waiting for transfers between devices  123 us (38%)
  local copies, waits for them, and re-layouts  73.3 us (23%)
  blocking collectives  50.2 us (15%)
  other arithmetic  25.8 us (8%)
  matrix products  25.7 us (8%)
  between operations  21.7 us (7%)
  starting transfers between devices  3.56 us (1%)
    psum x1, waiting for transfers between devices, local(): summed = lax.psum(packed, ('tm', 'cal'))  123 us
    all_gather x1, blocking collectives, jax.lax.all_gather(vals, axis_name=('tm', 'cal')).sum(axis=0)  42.5 us
    eq x1, local copies, waits for them, and re-layouts, local(): knot_hot = (local_knot[None] == knot_iota).astype(jnp.float32)  38.6 us
    eq x1, local copies, waits for them, and re-layouts, local(): high[None] == lax.broadcasted_iota(jnp.int32, (rows, 1, 1), 0)  20.5 us
    dot_general x1, matrix products, local(): jnp.einsum('hso,lso->hl', high_hot, cal_weighted, precision=EXACT)  11.2 us
    mul x1, local copies, waits for them, and re-layouts, local(): cal_weighted = (cal_design * weighted)[None] * low_hot  9.32 us
    dot_general x1, matrix products, local(): row_vals = jnp.einsum('hl,hso->lso', cal_table, high_hot, precision=EXACT)  8.24 us
    all_gather x1, blocking collectives, local(): cal_values = lax.all_gather(cal_dir, 'cal', axis=0, tiled=True)  7.65 us
  transfers between devices with their start and end apart: 3, of which 1 were waited for; matrix products, arithmetic and copies ran while one was open for 34% of the time, Pallas kernels for 0%

profile of v1, /device:TPU:0, one launch (start us, length us, event | category | flops | bytes accessed | tf_op | source)
XLA Modules:
  0.0 323.6 jit_solution(1761260230932469994)
XLA Ops:
  7.2 1.3 collective-permute-start
  8.5 0.6 compare_reduce_fusion.1
  9.2 0.6 compare_reduce_fusion
  9.8 0.7 constant_dynamic-update-slice_fusion.1
  10.5 1.4 multiply_reduce_fusion.4
  11.9 1.3 multiply_reduce_fusion.8
  13.2 1.3 multiply_reduce_fusion.6
  17.7 0.8 broadcast_subtract_fusion
  18.6 7.7 %all-gather.1 = f32[4,2,4096]{2,1,0:T(2,128)S(1)} all-gather(f32[1,2,4096]{2,1,0:T(2,128)} %bitcast.81), channel_id=1, replica_groups=mesh['tm'=8,'cal'=4] {'cal'}, dimensions={0}, use_global_device_ids=true | all-gather | bytes 163840 | tf_op jit(solution)/shard_map/all_gather | solution.py:52
  26.4 0.9 add_select_fusion.1
  27.4 1.3 iota_compare_fusion.1
  28.7 38.6 %copy.50 = pred[128,128,128]{2,0,1:T(32,128)(4,1)S(1)} copy(pred[128,128,128]{1,0,2:T(32,128)(4,1)S(1)} %iota_compare_fusion.1) | data formatting | bytes 4194304 | tf_op jit(solution)/shard_map/eq | solution.py:61
  67.3 2.7 iota_compare_fusion
  70.0 20.5 %copy.55 = pred[256,128,128]{2,0,1:T(32,128)(4,1)} copy(pred[256,128,128]{1,0,2:T(32,128)(4,1)S(1)} %iota_compare_fusion) | data formatting | bytes 8388608 | tf_op jit(solution)/shard_map/eq | solution.py:73
  90.8 8.2 %fusion = f32[128,128]{1,0:T(8,128)S(1)} fusion(s32[128,128]{1,0:T(8,128)S(1)} %get-tuple-element.62, pred[256,128,128]{2,0,1:T(32,128)(4,1)} %copy.55, f32[256,128]{1,0:T(8,128)S(1)} %reshape.141), kind=kOutput, calls=%fused_computation.2 | convolution fusion | flops 6448726016 | bytes 4456448 | tf_op jit(solution)/shard_map/hl,hso->lso/dot_general | solution.py:76
  99.2 2.1 fusion.29
  101.3 0.8 fusion.7
  102.9 4.2 %fusion.4 = f32[128,4,3]{0,1,2:T(4,128)S(1)} fusion(f32[4,3,128,128]{3,0,2,1:T(4,128)S(1)} %copy.59, s32[128,128]{0,1:T(8,128)S(1)} %copy.49), kind=kOutput, calls=%fused_computation.9 | convolution fusion | flops 304087040 | bytes 858112 | tf_op jit(solution)/shard_map/qso,jso->jq/dot_general | solution.py:92
  107.9 2.2 collective-permute-start.1
  110.2 4.7 %fusion.1 = f32[128,128,128]{2,0,1:T(8,128)} fusion(f32[128,128]{1,0:T(8,128)S(1)} %get-tuple-element.52, s32[128,128]{1,0:T(8,128)S(1)} %get-tuple-element.62), kind=kLoop, calls=%fused_computation.5 | loop fusion | flops 4194304 | bytes 8519680 | tf_op jit(solution)/shard_map/mul | solution.py:100
  114.9 9.3 %copy.57 = f32[128,128,128]{1,0,2:T(8,128)} copy(f32[128,128,128]{2,0,1:T(8,128)} %fusion.1) | data formatting | bytes 16777216 | tf_op jit(solution)/shard_map/mul | solution.py:100
  124.2 11.2 %convolution_bitcast_fusion = f32[256,128]{1,0:T(8,128)S(1)} fusion(f32[128,128,128]{1,0,2:T(8,128)} %copy.57, s32[128,128]{0,1:T(8,128)S(1)} %copy.48), kind=kOutput, calls=%fused_computation.8 | convolution fusion | flops 6446645248 | bytes 8585216 | tf_op jit(solution)/shard_map/hso,lso->hl/dot_general | solution.py:101
  135.4 2.5 fusion.28
  137.9 1.4 scatter.11
  139.3 0.7 pad_maximum_fusion
  140.0 123.3 %all-reduce.8.cloned.1.call-done = f32[257,128]{1,0:T(8,128)} async-done(((f32[257,128]{1,0:T(8,128)}), f32[257,128]{1,0:T(8,128)}) %all-reduce.8.cloned.1.call-update) | async-done | bytes 131600 | tf_op jit(solution)/shard_map/psum | solution.py:104
  263.3 1.3 fusion.26
  266.0 0.8 dynamic-slice_multiply_fusion
  267.4 0.7 multiply_reduce_fusion.3
  268.9 0.8 multiply_reduce_fusion.7
  271.6 42.5 %all-gather.2 = f32[32,1,128]{2,1,0:T(1,128)S(1)} all-gather(f32[1,1,128]{2,1,0:T(1,128)S(1)} %pad_bitcast_fusion), channel_id=2, replica_groups=mesh['tm'=8,'cal'=4] {'tm','cal'}, dimensions={0}, use_global_device_ids=true | all-gather | bytes 16896 | tf_op jit(solution)/shard_map/all_gather | solution.py:7
  316.1 0.6 multiply_add_fusion.1
  (64 shorter events, 4.6 us)
Async XLA Ops:
  7.2 256.2 %all-reduce.8.cloned.1.call-start = ((), (), s32[]{:S(2)}) async-start(), calls=%async_computation | async-start | bytes 270336 | tf_op jit(solution)/shard_map/psum | solution.py:104
  7.2 91.8 %collective-permute-start = (f32[3,3]{1,0:T(4,128)}, f32[3,3]{1,0:T(4,128)S(1)}, u32[]{:S(2)}, u32[]{:S(2)}) collective-permute-start(f32[3,3]{1,0:T(4,128)} %bitcast.82), channel_id=1, source_target_pairs={{1,0},{2,1},{3,2},{4,3},{5,4},{6,5},{7,6},{8,7},{9,8},{10,9},{11,1... | collective-permute-start | bytes 116 | tf_op jit(solution)/shard_map/ppermute | solution.py:13
  70.0 20.6 %copy-start = (f32[5,128,128]{2,1,0:T(8,128)S(1)}, f32[5,128,128]{2,1,0:T(8,128)}, u32[]{:S(2)}) copy-start(f32[5,128,128]{2,1,0:T(8,128)} %param.21) | copy-start | bytes 983044
  70.0 20.6 %copy-start.9 = (f32[5,128]{1,0:T(8,128)S(1)}, f32[5,128]{1,0:T(8,128)}, u32[]{:S(2)}) copy-start(f32[5,128]{1,0:T(8,128)} %param.33) | copy-start | bytes 7684
  90.7 8.4 %copy-start.8 = (f32[3,128]{1,0:T(4,128)S(1)}, f32[3,128]{1,0:T(4,128)}, u32[]{:S(2)}) copy-start(f32[3,128]{1,0:T(4,128)} %param.34) | copy-start | bytes 4612
  90.7 10.6 %copy-start.1 = (f32[3,128,128]{2,1,0:T(8,128)S(1)}, f32[3,128,128]{2,1,0:T(8,128)}, u32[]{:S(2)}) copy-start(f32[3,128,128]{2,1,0:T(8,128)} %param.22) | copy-start | bytes 589828
  99.0 3.2 copy-start.5
  99.0 3.2 copy-start.6
  99.0 3.2 copy-start.7
  99.0 3.2 copy-start.14
  107.9 32.1 %collective-permute-start.1 = (f32[3,3]{1,0:T(4,128)S(1)}, f32[3,3]{1,0:T(4,128)S(1)}, u32[]{:S(2)}, u32[]{:S(2)}) collective-permute-start(f32[3,3]{1,0:T(4,128)S(1)} %slice.142), channel_id=1, source_target_pairs={{0,1},{1,2},{2,3},{3,4},{4,5},{5,6},{6,7},{7,8},{8,9},{9,10},{10,1... | collective-permute-start | bytes 116 | tf_op jit(solution)/shard_map/ppermute | solution.py:13
  124.2 142.6 %copy-start.11 = (f32[5,128]{1,0:T(8,128)S(1)}, f32[5,128]{1,0:T(8,128)}, u32[]{:S(2)}) copy-start(f32[5,128]{1,0:T(8,128)} %param.30) | copy-start | bytes 7684
  124.2 143.2 %copy-start.4 = (f32[2,4096]{1,0:T(2,128)S(1)}, f32[2,4096]{1,0:T(2,128)}, u32[]{:S(2)}) copy-start(f32[2,4096]{1,0:T(2,128)} %param.32) | copy-start | bytes 98308
  124.2 144.6 %copy-start.12 = (f32[3,128]{1,0:T(4,128)S(1)}, f32[3,128]{1,0:T(4,128)}, u32[]{:S(2)}) copy-start(f32[3,128]{1,0:T(4,128)} %param.31) | copy-start | bytes 4612
  124.2 191.9 %copy-start.2 = (f32[2,4096]{1,0:T(2,128)S(1)}, f32[2,4096]{1,0:T(2,128)}, u32[]{:S(2)}) copy-start(f32[2,4096]{1,0:T(2,128)} %param.35) | copy-start | bytes 98308
  267.4 49.3 %copy-start.10 = (f32[5,128]{1,0:T(8,128)}, f32[5,128]{1,0:T(8,128)S(1)}, u32[]{:S(2)}) copy-start(f32[5,128]{1,0:T(8,128)S(1)} %get-tuple-element.51) | copy-start | bytes 7684
  268.2 48.6 %copy-start.3 = (f32[2,4096]{1,0:T(2,128)}, f32[2,4096]{1,0:T(2,128)S(1)}, u32[]{:S(2)}) copy-start(f32[2,4096]{1,0:T(2,128)S(1)} %get-tuple-element.47) | copy-start | bytes 98308
  269.6 47.1 %copy-start.13 = (f32[3,128]{1,0:T(4,128)}, f32[3,128]{1,0:T(4,128)S(1)}, u32[]{:S(2)}) copy-start(f32[3,128]{1,0:T(4,128)S(1)} %get-tuple-element.49) | copy-start | bytes 4612
Sparse Core Ops, SparseCore 0:
  140.1 123.1 all-reduce.7
